TPU v7x, 128 devices: a whole 4x4x4 slice. The times are simulated.
128 devices in a mesh: req: 16 (over y, z), mp: 8 (over x, core).
Axes of the slice: x: 4, y: 4, z: 4, core: 2. Of those that a mesh axis runs over, the one named last changes fastest.
Arguments:
- hidden_in: bfloat16 [16384, 2048], P('req', 'mp'), may hold values from -6 to 6
- w_qkv: bfloat16 [3, 2048, 2048], P(None, 'req', 'mp'), may hold values from -0.125 to 0.125
- w_out: bfloat16 [2048, 2048], P('mp', 'req'), may hold values from -0.125 to 0.125
- attn_gain: bfloat16 [2048], replicated, may hold values from 0.099609375 to 1.8984375
- mlp_gain: bfloat16 [2048], replicated, may hold values from 0.099609375 to 1.8984375
- w_gate: bfloat16 [2048, 8192], P('req', 'mp'), may hold values from -0.125 to 0.125
- w_up: bfloat16 [2048, 8192], P('req', 'mp'), may hold values from -0.125 to 0.125
- w_down: bfloat16 [8192, 2048], P('mp', 'req'), may hold values from -0.0625 to 0.0625
- k_cache: bfloat16 [16, 4096, 2048], P('req', None, 'mp'), may hold values from -363 to 363
- v_cache: bfloat16 [16, 4096, 2048], P('req', None, 'mp'), may hold values from -6 to 6
- cache_len: int32 [16], P('req'), may hold values from 256 to 4096, as said below
Outputs:
- hidden_out: bfloat16 [16384, 2048], P('req', 'mp')
- new_keys: bfloat16 [16384, 2048], P('req', 'mp')
- new_values: bfloat16 [16384, 2048], P('req', 'mp')
Inputs may be any that keep to these rules, and one draw needn't show every extreme that they name: Each request uses its first cache_len slots; later slots hold unused data. Some request's cache is full in every draw.
All inputs are finite; a program needn't handle non-finite values.
Results may differ from a plain program's by a relative error of at most 0.02.
Values may be sent and summed in bfloat16 or wider, within the bound.
No kernel may reach another device: no remote copies, remote signals or barrier semaphores. Data moves between devices by JAX's collectives and lax.ppermute only.
A program may use at most 128 MiB of HBM per device.

v0:
```python
import jax
import jax.numpy as jnp
from jax import lax
from jax.sharding import PartitionSpec as P

HD = 64
THETA = 130000.0
EPSILON = 1e-05
NEG_FILL = -1e30


def rms_scale(rows, gain):
    values = rows.astype(jnp.float32)
    meansq = jnp.mean(values * values, axis=-1, keepdims=True)
    return (values * lax.rsqrt(meansq + EPSILON) * gain.astype(jnp.float32)).astype(jnp.bfloat16)


def rotate(tensor, positions):
    half = tensor.shape[-1] // 2
    freq = THETA ** (-(jnp.arange(half, dtype=jnp.float32) * 2.0 / tensor.shape[-1]))
    angle = positions[:, None, None] * freq[None, None, :]
    cosine = jnp.cos(angle)
    sine = jnp.sin(angle)
    first = tensor[..., :half]
    second = tensor[..., half:]
    return jnp.concatenate(
        [first * cosine - second * sine, second * cosine + first * sine], axis=-1
    )


def gather_packed(blocks, axes, axis_name):
    count = lax.axis_size(axis_name)
    lane = 128
    joined = jnp.concatenate([block.reshape(-1, lane) for block in blocks], axis=0)
    gathered = lax.all_gather(joined, axis_name, axis=0, tiled=False)
    outs = []
    offset = 0
    for block, axis in zip(blocks, axes):
        rows = block.size // lane
        piece = gathered[:, offset : offset + rows].reshape((count,) + block.shape)
        piece = jnp.moveaxis(piece, 0, axis)
        shape = list(block.shape)
        shape[axis] *= count
        outs.append(piece.reshape(shape))
        offset += rows
    return outs


def absorb(carry, queries, keys, values, valid):
    top, total, accum = carry
    scores = jnp.einsum("qhd,khd->hqk", queries, keys, preferred_element_type=jnp.float32) * HD ** (
        -0.5
    )
    scores = jnp.where(valid[None], scores, NEG_FILL)
    new_top = jnp.maximum(top, jnp.max(scores, axis=-1, keepdims=True))
    factor = jnp.exp(top - new_top)
    probs = jnp.where(valid[None], jnp.exp(scores - new_top), 0.0)
    total = total * factor + jnp.sum(probs, axis=-1, keepdims=True)
    accum = accum * factor + jnp.einsum(
        "hqk,khd->hqd", probs.astype(jnp.bfloat16), values, preferred_element_type=jnp.float32
    )
    return (new_top, total, accum)


def on_device(
    hidden_in, w_qkv, w_out, attn_gain, mlp_gain, w_gate, w_up, w_down, k_cache, v_cache, cache_len
):
    new_count = hidden_in.shape[0]
    w_qkv_full = lax.all_gather(w_qkv, "req", axis=1, tiled=True)
    w_gate_full, w_up_full, w_down_full, w_out_full = gather_packed(
        [w_gate, w_up, w_down, w_out], [0, 0, 1, 1], "req"
    )
    width = w_qkv.shape[2]
    heads_local = width // HD
    slots = k_cache.shape[1]
    full_rows = lax.all_gather(hidden_in, "mp", axis=1, tiled=True)
    normed = rms_scale(full_rows, attn_gain)
    columns = normed
    projected = jnp.einsum("nd,kdw->knw", columns, w_qkv_full, preferred_element_type=jnp.float32)
    length = cache_len[0]
    positions = (length + jnp.arange(new_count, dtype=jnp.int32)).astype(jnp.float32)
    queries = rotate(projected[0].reshape(new_count, heads_local, HD), positions).astype(
        jnp.bfloat16
    )
    fresh_keys = rotate(projected[1].reshape(new_count, heads_local, HD), positions).astype(
        jnp.bfloat16
    )
    fresh_values = projected[2].astype(jnp.bfloat16).reshape(new_count, heads_local, HD)
    rows = jnp.arange(new_count, dtype=jnp.int32)
    causal = rows[:, None] >= rows[None, :]
    start_carry = (
        jnp.full((heads_local, new_count, 1), NEG_FILL, jnp.float32),
        jnp.zeros((heads_local, new_count, 1), jnp.float32),
        jnp.zeros((heads_local, new_count, HD), jnp.float32),
    )
    carry = absorb(start_carry, queries, fresh_keys, fresh_values, causal)
    cache_keys = k_cache[0].reshape(slots, heads_local, HD)
    cache_values = v_cache[0].reshape(slots, heads_local, HD)
    block = min(slots, 512)
    count = (length + block - 1) // block

    def step_block(index, state):
        begin = index * block
        keys = lax.dynamic_slice_in_dim(cache_keys, begin, block, 0)
        values = lax.dynamic_slice_in_dim(cache_values, begin, block, 0)
        valid = (begin + jnp.arange(block, dtype=jnp.int32) < length)[None, :]
        return absorb(state, queries, keys, values, valid)

    top, total, accum = lax.fori_loop(0, count, step_block, carry)
    attn = (accum / total).transpose(1, 0, 2).reshape(new_count, width).astype(jnp.bfloat16)
    partial_value = jnp.dot(attn, w_out_full, preferred_element_type=jnp.float32)
    summed = lax.psum(partial_value.astype(jnp.bfloat16), "mp").astype(jnp.float32)
    mid_full = (full_rows.astype(jnp.float32) + summed).astype(jnp.bfloat16)
    own = hidden_in.shape[1]
    mid_local = lax.dynamic_slice_in_dim(mid_full, lax.axis_index("mp") * own, own, axis=1)
    normed2 = rms_scale(mid_full, mlp_gain)
    columns = normed2
    gate = jnp.dot(columns, w_gate_full, preferred_element_type=jnp.float32)
    upper = jnp.dot(columns, w_up_full, preferred_element_type=jnp.float32)
    units = (jax.nn.silu(gate) * upper).astype(jnp.bfloat16)
    terms = jnp.dot(units, w_down_full, preferred_element_type=jnp.float32)
    reduced = lax.psum_scatter(
        terms.astype(jnp.bfloat16), "mp", scatter_dimension=1, tiled=True
    ).astype(jnp.float32)
    hidden_out = (mid_local.astype(jnp.float32) + reduced).astype(jnp.bfloat16)
    return (
        hidden_out,
        fresh_keys.reshape(new_count, width),
        fresh_values.reshape(new_count, width),
    )


def solution(mesh):
    return jax.shard_map(
        on_device,
        mesh=mesh,
        in_specs=(
            P("req", "mp"),
            P(None, "req", "mp"),
            P("mp", "req"),
            P(),
            P(),
            P("req", "mp"),
            P("req", "mp"),
            P("mp", "req"),
            P("req", None, "mp"),
            P("req", None, "mp"),
            P("req"),
        ),
        out_specs=(P("req", "mp"), P("req", "mp"), P("req", "mp")),
        check_vma=False,
    )
```

profile of v0, /device:TPU:0, one launch (start us, length us, event | category | flops | bytes accessed | tf_op | source)
XLA Modules:
  0.0 353.1 jit_solution(15132475671423839923)
XLA Ops:
  8.0 1.7 copy.29
  9.8 1.1 reshape.167
  11.9 2.0 pad_maximum_fusion
  14.6 2.9 copy.31
  17.6 4.1 %copy.32 = bf16[1,4096,256]{1,2,0:T(8,128)(2,1)} copy(bf16[1,4096,256]{2,1,0:T(8,128)(2,1)} %param.22) | data formatting | bytes 4194304 | tf_op args[9]
  21.7 1.3 iota_compare_fusion
  23.5 24.7 %all-gather.5.cloned.1.call-done = bf16[1024,2048]{1,0:T(8,128)(2,1)} async-done(((bf16[1024,256]{1,0:T(8,128)(2,1)}), bf16[1024,2048]{1,0:T(8,128)(2,1)}) %all-gather.5.cloned.1.call-update) | async-done | bytes 4194320 | tf_op jit(solution)/shard_map/all_gather | solution.py:76
  48.2 3.1 fusion.26
  51.3 53.4 %all-gather.7.cloned.1.call-done = bf16[3,2048,256]{1,2,0:T(8,128)(2,1)} async-done(((bf16[3,128,256]{1,2,0:T(8,128)(2,1)}), bf16[3,2048,256]{1,2,0:T(8,128)(2,1)}) %all-gather.7.cloned.1.call-update) | async-done | bytes 3145744 | tf_op jit(solution)/shard_map/all_gather | solution.py:69
  104.7 6.6 %fusion.38 = f32[3,1024,256]{1,2,0:T(8,128)S(1)} fusion(bf16[3,2048,256]{1,2,0:T(8,128)(2,1)} %all-gather.7.cloned.1.call-done, bf16[1024,2048]{1,0:T(8,128)(2,1)} %all-gather.5.cloned.1.call-done, f32[2048]{0:T(1024)S(1)} %convert_element_type.84, f32[1024]{0:T(1024)S(1)} %add_rsqrt_fusion.1), kind=kOutput, calls=%fused_computation.52 | convolution fusion | flops 3229614080 | bytes 10498048 | tf_op jit(solution)/shard_map/nd,kdw->knw/dot_general | solution.py:79
  113.8 3.0 fusion.20
  116.8 4.2 %fusion.22 = f32[4,1024]{1,0:T(4,128)S(1)} fusion(f32[4,1024,1024]{1,2,0:T(8,128)S(1)} %get-tuple-element.102, f32[4,1024]{1,0:T(4,128)S(1)} %get-tuple-element.98, pred[1024,1024]{0,1:T(8,128)(4,1)S(1)} %copy-done.1), kind=kLoop, calls=%fused_computation.31 | loop fusion | flops 20967424 | bytes 17858560 | tf_op jit(solution)/shard_map/reduce_sum | solution.py:58
  121.1 5.9 %fusion.41 = f32[4,1024,64]{1,2,0:T(8,128)} fusion(bf16[1024,4,64]{0,2,1:T(8,128)(2,1)S(1)} %bitcast.91, f32[4,1024,1024]{1,2,0:T(8,128)S(1)} %get-tuple-element.102, f32[4,1024]{1,0:T(4,128)S(1)} %get-tuple-element.98, pred[1024,1024]{0,1:T(8,128)(4,1)S(1)} %copy-done.1, f32[4,1024]{1,0:T(4,128)S(1)} %get-tuple-element.96), kind=kOutput, calls=%fused_computation.53 | convolution fusion | flops 558104576 | bytes 19431424 | tf_op jit(solution)/shard_map/hqk,khd->hqd/dot_general | solution.py:59
  127.0 8.0 %while.14 = (s32[]{:T(128)}, f32[4,1024,1]{1,0,2:T(4,128)S(1)}, f32[4,1024,1]{1,0,2:T(4,128)S(1)}, f32[4,1024,64]{1,2,0:T(8,128)}, s32[]{:T(128)}, /*index=5*/s3...) while((s32[]{:T(128)}, f32[4,1024,1]{1,0,2:T(4,128)S(1)}, ...), condition=%wide.region_6.7_spmd, body=%wide.region_3.6_spmd.sunk | while | flops 564671488 | bytes 36965104 | solution.py:109
  127.7 1.6 bitcast_reduce_fusion.2
  129.3 3.1 fusion.77
  132.4 2.5 fusion.76
  135.0 1.3 divide_convert_fusion
  136.3 65.2 %all-gather.9.cloned.1.call-done = bf16[53248,128]{1,0:T(8,128)(2,1)} async-done(((bf16[3328,128]{1,0:T(8,128)(2,1)}), bf16[53248,128]{1,0:T(8,128)(2,1)}) %all-gather.9.cloned.1.call-update) | async-done | bytes 13631504 | tf_op jit(solution)/shard_map/all_gather | solution.py:35
  201.5 1.3 slice_bitcast_fusion.1
  203.4 3.3 convolution_convert_fusion
  207.4 9.1 %fusion.56 = (bf16[16,1024,128]{2,1,0:T(8,128)(2,1)}, bf16[1024,16,128]{2,0,1:T(8,128)(2,1)}, bf16[16,1024,128]{2,1,0:T(8,128)(2,1)}) fusion(bf16[16,3328,128]{2,1,0:T(8,128)(2,1)} %bitcast.79), kind=kLoop, calls=%fused_computation.81 | loop fusion | bytes 25165824 | tf_op jit(solution)/shard_map/slice | solution.py:40
  216.5 7.4 %reshape_reshape.6 = bf16[2048,1024]{1,0:T(8,128)(2,1)} reshape(bf16[16,1024,128]{2,1,0:T(8,128)(2,1)} %get-tuple-element.89) | data formatting | bytes 8388608 | tf_op jit(solution)/shard_map/reshape;reshape | solution.py:44
  223.9 6.4 %copy.34 = bf16[1024,16,128]{0,2,1:T(8,128)(2,1)} copy(bf16[1024,16,128]{2,0,1:T(8,128)(2,1)} %get-tuple-element.88) | data formatting | bytes 8388608 | tf_op jit(solution)/shard_map/transpose | solution.py:41
  230.4 7.4 %reshape_reshape.7 = bf16[2048,1024]{1,0:T(8,128)(2,1)} reshape(bf16[16,1024,128]{2,1,0:T(8,128)(2,1)} %get-tuple-element.87) | data formatting | bytes 8388608 | tf_op jit(solution)/shard_map/reshape;reshape | solution.py:44
  237.8 41.3 %all-reduce.2.cloned.1.call-done = bf16[1024,2048]{1,0:T(8,128)(2,1)} async-done(((bf16[1024,2048]{1,0:T(8,128)(2,1)}), bf16[1024,2048]{1,0:T(8,128)(2,1)}) %all-reduce.2.cloned.1.call-update) | async-done | bytes 4194320 | tf_op jit(solution)/shard_map/psum | solution.py:112
  279.0 5.6 %fusion.23 = (f32[1024]{0:T(1024)S(1)}, bf16[1024,2048]{1,0:T(8,128)(2,1)S(1)}) fusion(bf16[1024,2048]{1,0:T(8,128)(2,1)} %all-reduce.2.cloned.1.call-done, bf16[1024,2048]{1,0:T(8,128)(2,1)} %all-gather.5.cloned.1.call-done), kind=kLoop, calls=%fused_computation.34 | loop fusion | flops 14679040 | bytes 12587008 | tf_op jit(solution)/shard_map/reduce_sum | solution.py:14
  284.7 6.3 %fusion.45 = f32[1024,1024]{1,0:T(8,128)} fusion(bf16[2048,1024]{1,0:T(8,128)(2,1)S(1)} %copy-done.2, bf16[1024,2048]{1,0:T(8,128)(2,1)S(1)} %get-tuple-element.84, f32[2048]{0:T(1024)S(1)} %convert_element_type.99, f32[1024]{0:T(1024)S(1)} %add_rsqrt_fusion), kind=kOutput, calls=%fused_computation.54 | convolution fusion | flops 4303355904 | bytes 12595200 | tf_op jit(solution)/shard_map/dot_general | solution.py:118
  291.0 15.4 %convolution_convert_fusion.1 = bf16[1024,2048]{1,0:T(8,128)(2,1)} fusion(bf16[1024,2048]{0,1:T(8,128)(2,1)} %bitcast.84, f32[1024,1024]{1,0:T(8,128)} %fusion.45, bf16[2048,1024]{1,0:T(8,128)(2,1)} %reshape_reshape.7, bf16[1024,2048]{1,0:T(8,128)(2,1)} %copy-done, f32[2048]{0:T(1024)S(1)} %convert_element_type.99, f32[1024]{0:T(1024)S(1)} %add_rsqrt_fusion), kind=kOutput, calls=%fused_computation.51 | convolution fusion | flops 8606711808 | bytes 20983808 | tf_op jit(solution)/shard_map/dot_general | solution.py:121
  307.4 1.3 slice_bitcast_fusion.2
  309.7 34.8 %reduce-scatter.2.cloned.1.call-done = bf16[1024,256]{1,0:T(8,128)(2,1)} async-done(((bf16[1024,2048]{1,0:T(8,128)(2,1)}), bf16[1024,256]{1,0:T(8,128)(2,1)}) %reduce-scatter.2.cloned.1.call-update) | async-done | bytes 524304 | tf_op jit(solution)/shard_map/reduce_scatter | solution.py:122
  344.5 2.1 add_convert_fusion
  (51 shorter events, 9.0 us)
Async XLA Ops:
  7.2 7.4 %copy-start.7 = (bf16[2048]{0:T(1024)(128)(2,1)S(1)}, bf16[2048]{0:T(1024)(128)(2,1)}, u32[]{:S(2)}) copy-start(bf16[2048]{0:T(1024)(128)(2,1)} %param.16) | copy-start | bytes 12292
  7.2 41.0 %all-gather.5.cloned.1.call-start = ((), (), s32[]{:S(2)}) async-start(), calls=%async_computation.1 | async-start | bytes 4718592 | tf_op jit(solution)/shard_map/all_gather | solution.py:76
  7.9 96.8 %all-gather.7.cloned.1.call-start = ((), (), s32[]{:S(2)}) async-start(), calls=%async_computation.2 | async-start | bytes 3342336 | tf_op jit(solution)/shard_map/all_gather | solution.py:69
  9.7 191.8 %all-gather.9.cloned.1.call-start = ((), (), s32[]{:S(2)}) async-start(), calls=%async_computation.5 | async-start | bytes 14483456 | tf_op jit(solution)/shard_map/all_gather | solution.py:35
  13.9 265.1 %all-reduce.2.cloned.1.call-start = ((), (), s32[]{:S(2)}) async-start(), calls=%async_computation.3 | async-start | bytes 8388608 | tf_op jit(solution)/shard_map/psum | solution.py:112
  111.3 1.8 copy-start.3
  112.3 1.5 copy-start.1
  116.8 4.2 %copy-start.6 = (bf16[1,1024,256]{1,2,0:T(8,128)(2,1)S(1)}, bf16[1,1024,256]{1,2,0:T(8,128)(2,1)}, u32[]{:S(2)}) copy-start(bf16[1,1024,256]{1,2,0:T(8,128)(2,1)} %slice.66) | copy-start | bytes 1572868
  127.7 1.6 copy-start.4
  132.4 2.6 copy-start.5
  206.7 0.7 copy-start.8
  206.7 137.7 %reduce-scatter.2.cloned.1.call-start = ((), (), s32[]{:S(2)}) async-start(), calls=%async_computation.4 | async-start | bytes 4718592 | tf_op jit(solution)/shard_map/reduce_scatter | solution.py:122
  279.0 5.6 %copy-start.2 = (bf16[2048,1024]{1,0:T(8,128)(2,1)S(1)}, bf16[2048,1024]{1,0:T(8,128)(2,1)}, u32[]{:S(2)}) copy-start(bf16[2048,1024]{1,0:T(8,128)(2,1)} %reshape_reshape.6) | copy-start | bytes 12582916
  284.6 6.4 %copy-start = (bf16[1024,2048]{1,0:T(8,128)(2,1)}, bf16[1024,2048]{1,0:T(8,128)(2,1)S(1)}, u32[]{:S(2)}) copy-start(bf16[1024,2048]{1,0:T(8,128)(2,1)S(1)} %get-tuple-element.84) | copy-start | bytes 12582916
Sparse Core Ops, SparseCore 0:
  9.7 38.4 all-gather.4
  50.9 53.7 all-gather.6
  106.9 94.6 all-gather.8
  206.9 72.1 all-reduce.1
  306.5 37.9 reduce-scatter.1
where the time goes:
time: 354 us; the launch traced here: 353 us
  waiting for transfers between devices  220 us (62%)
  local copies, waits for them, and re-layouts  48.9 us (14%)
  matrix products  45.3 us (13%)
  other arithmetic  23.8 us (7%)
  between operations  14.7 us (4%)
    all_gather x1, waiting for transfers between devices, gather_packed(): gathered = lax.all_gather(joined, axis_name, axis=0, tiled=False)  65.2 us
    all_gather x1, waiting for transfers between devices, on_device(): w_qkv_full = lax.all_gather(w_qkv, 'req', axis=1, tiled=True)  53.4 us
    psum x1, waiting for transfers between devices, on_device(): lax.psum(partial_value.astype(jnp.bfloat16), 'mp').astype(jnp.float32)  41.3 us
    reduce_scatter x1, waiting for transfers between devices, on_device(): lax.psum_scatter(terms.astype(jnp.bfloat16), 'mp', scatter_dimension=1, t...  34.8 us
    all_gather x1, waiting for transfers between devices, on_device(): full_rows = lax.all_gather(hidden_in, 'mp', axis=1, tiled=True)  24.7 us
    dot_general x1, matrix products, on_device(): terms = jnp.dot(units, w_down_full, preferred_element_type=jnp.float32)  15.4 us
    another operation x2, local copies, waits for them, and re-layouts, gather_packed(): outs.append(piece.reshape(shape))  14.8 us
    unnamed x19, local copies, waits for them, and re-layouts  12.2 us
  transfers between devices with their start and end apart: 5, of which 5 were waited for; matrix products, arithmetic and copies ran while one was open for 23% of the time, Pallas kernels for 0%

commit v1 on v0

--- a/solution.py
+++ b/solution.py
@@ -109,7 +109,9 @@
     top, total, accum = lax.fori_loop(0, count, step_block, carry)
     attn = (accum / total).transpose(1, 0, 2).reshape(new_count, width).astype(jnp.bfloat16)
     partial_value = jnp.dot(attn, w_out_full, preferred_element_type=jnp.float32)
-    summed = lax.psum(partial_value.astype(jnp.bfloat16), "mp").astype(jnp.float32)
+    summed = jnp.sum(lax.all_gather(partial_value.astype(jnp.bfloat16), "mp"), axis=0).astype(
+        jnp.float32
+    )
     mid_full = (full_rows.astype(jnp.float32) + summed).astype(jnp.bfloat16)
     own = hidden_in.shape[1]
     mid_local = lax.dynamic_slice_in_dim(mid_full, lax.axis_index("mp") * own, own, axis=1)

time: 354 us -> 453 us (1.28)
  waiting for transfers between devices: 220 us -> 302 us
  other arithmetic: 23.8 us -> 38 us
    all_gather x0 -> x1, waiting for transfers between devices: none -> 124 us  [on_device(): lax.all_gather(partial_value.astype(jnp.bfloat16), 'mp')]
    psum x1 -> x0, waiting for transfers between devices: 41.3 us -> none  [on_device(): lax.psum(partial_value.astype(jnp.bfloat16), 'mp').astype(jnp.float32)]
    reduce_sum x0 -> x1, other arithmetic: none -> 14.2 us  [on_device(): jnp.sum(lax.all_gather(partial_value.astype(jnp.bfloat16), 'mp'), axis=0)]
  transfers between devices with their start and end apart: 5 -> 5, of which waited for: 5 -> 5; matrix products, arithmetic and copies ran while one was open for 23% -> 18% of each run, Pallas kernels for 0% -> 0%
where the time goes in v1:
time: 453 us; the launch traced here: 452 us
  waiting for transfers between devices  302 us (67%)
  local copies, waits for them, and re-layouts  50.7 us (11%)
  matrix products  45.4 us (10%)
  other arithmetic  38 us (8%)
  between operations  14.7 us (3%)
    all_gather x1, waiting for transfers between devices, on_device(): lax.all_gather(partial_value.astype(jnp.bfloat16), 'mp')  124 us
    all_gather x1, waiting for transfers between devices, gather_packed(): gathered = lax.all_gather(joined, axis_name, axis=0, tiled=False)  64.2 us
    all_gather x1, waiting for transfers between devices, on_device(): w_qkv_full = lax.all_gather(w_qkv, 'req', axis=1, tiled=True)  53.4 us
    reduce_scatter x1, waiting for transfers between devices, on_device(): lax.psum_scatter(terms.astype(jnp.bfloat16), 'mp', scatter_dimension=1, t...  35.6 us
    all_gather x1, waiting for transfers between devices, on_device(): full_rows = lax.all_gather(hidden_in, 'mp', axis=1, tiled=True)  24.7 us
    dot_general x1, matrix products, on_device(): terms = jnp.dot(units, w_down_full, preferred_element_type=jnp.float32)  15.4 us
    another operation x2, local copies, waits for them, and re-layouts, gather_packed(): outs.append(piece.reshape(shape))  15.1 us
    reduce_sum x1, other arithmetic, on_device(): jnp.sum(lax.all_gather(partial_value.astype(jnp.bfloat16), 'mp'), axis=0)  14.2 us
  transfers between devices with their start and end apart: 5, of which 5 were waited for; matrix products, arithmetic and copies ran while one was open for 18% of the time, Pallas kernels for 0%

profile of v1, /device:TPU:0, one launch (start us, length us, event | category | flops | bytes accessed | tf_op | source)
XLA Modules:
  0.0 451.6 jit_solution(3264592087518505199)
XLA Ops:
  8.0 1.7 copy.29
  11.9 1.9 pad_maximum_fusion
  14.6 2.9 copy.31
  17.5 4.1 copy.32
  21.7 1.3 iota_compare_fusion
  23.5 24.7 %all-gather.7.cloned.1.call-done = bf16[1024,2048]{1,0:T(8,128)(2,1)} async-done(((bf16[1024,256]{1,0:T(8,128)(2,1)}), bf16[1024,2048]{1,0:T(8,128)(2,1)}) %all-gather.7.cloned.1.call-update) | async-done | bytes 4194320 | tf_op jit(solution)/shard_map/all_gather | solution.py:76
  48.2 3.1 fusion.26
  51.3 53.4 %all-gather.9.cloned.1.call-done = bf16[3,2048,256]{1,2,0:T(8,128)(2,1)} async-done(((bf16[3,128,256]{1,2,0:T(8,128)(2,1)}), bf16[3,2048,256]{1,2,0:T(8,128)(2,1)}) %all-gather.9.cloned.1.call-update) | async-done | bytes 3145744 | tf_op jit(solution)/shard_map/all_gather | solution.py:69
  104.7 6.6 %fusion.38 = f32[3,1024,256]{1,2,0:T(8,128)S(1)} fusion(bf16[3,2048,256]{1,2,0:T(8,128)(2,1)} %all-gather.9.cloned.1.call-done, bf16[1024,2048]{1,0:T(8,128)(2,1)} %all-gather.7.cloned.1.call-done, f32[2048]{0:T(1024)S(1)} %convert_element_type.86, f32[1024]{0:T(1024)S(1)} %add_rsqrt_fusion.1), kind=kOutput, calls=%fused_computation.52 | convolution fusion | flops 3229614080 | bytes 10498048 | tf_op jit(solution)/shard_map/nd,kdw->knw/dot_general | solution.py:79
  113.8 3.0 fusion.20
  116.8 4.2 fusion.22
  121.1 6.0 %fusion.41 = f32[4,1024,64]{1,2,0:T(8,128)} fusion(bf16[1024,4,64]{0,2,1:T(8,128)(2,1)S(1)} %bitcast.93, f32[4,1024,1024]{1,2,0:T(8,128)S(1)} %get-tuple-element.102, f32[4,1024]{1,0:T(4,128)S(1)} %get-tuple-element.98, pred[1024,1024]{0,1:T(8,128)(4,1)S(1)} %copy-done.1, f32[4,1024]{1,0:T(4,128)S(1)} %get-tuple-element.96), kind=kOutput, calls=%fused_computation.53 | convolution fusion | flops 558104576 | bytes 19431424 | tf_op jit(solution)/shard_map/hqk,khd->hqd/dot_general | solution.py:59
  127.1 8.9 %while.14 = (s32[]{:T(128)}, f32[4,1024,1]{1,0,2:T(4,128)S(1)}, f32[4,1024,1]{1,0,2:T(4,128)S(1)}, f32[4,1024,64]{1,2,0:T(8,128)}, s32[]{:T(128)}, /*index=5*/s3...) while((s32[]{:T(128)}, f32[4,1024,1]{1,0,2:T(4,128)S(1)}, ...), condition=%wide.region_6.7_spmd, body=%wide.region_3.6_spmd.sunk | while | flops 564671488 | bytes 36965104 | solution.py:109
  127.8 1.6 bitcast_reduce_fusion.2
  129.4 2.5 fusion.76
  131.9 3.1 fusion.77
  136.0 1.3 divide_convert_fusion
  137.4 64.2 %all-gather.11.cloned.1.call-done = bf16[53248,128]{1,0:T(8,128)(2,1)} async-done(((bf16[3328,128]{1,0:T(8,128)(2,1)}), bf16[53248,128]{1,0:T(8,128)(2,1)}) %all-gather.11.cloned.1.call-update) | async-done | bytes 13631504 | tf_op jit(solution)/shard_map/all_gather | solution.py:35
  201.5 1.3 slice_bitcast_fusion.1
  203.4 3.4 convolution_convert_fusion
  207.4 9.4 %fusion.56 = (bf16[16,1024,128]{2,1,0:T(8,128)(2,1)}, bf16[1024,16,128]{2,0,1:T(8,128)(2,1)}, bf16[16,1024,128]{2,1,0:T(8,128)(2,1)}) fusion(bf16[16,3328,128]{2,1,0:T(8,128)(2,1)} %bitcast.81), kind=kLoop, calls=%fused_computation.81 | loop fusion | bytes 25165824 | tf_op jit(solution)/shard_map/slice | solution.py:40
  216.8 7.7 %reshape_reshape.7 = bf16[2048,1024]{1,0:T(8,128)(2,1)} reshape(bf16[16,1024,128]{2,1,0:T(8,128)(2,1)} %get-tuple-element.87) | data formatting | bytes 8388608 | tf_op jit(solution)/shard_map/reshape;reshape | solution.py:44
  224.5 6.7 %copy.34 = bf16[1024,16,128]{0,2,1:T(8,128)(2,1)} copy(bf16[1024,16,128]{2,0,1:T(8,128)(2,1)} %get-tuple-element.88) | data formatting | bytes 8388608 | tf_op jit(solution)/shard_map/transpose | solution.py:41
  231.2 7.4 %reshape_reshape.6 = bf16[2048,1024]{1,0:T(8,128)(2,1)} reshape(bf16[16,1024,128]{2,1,0:T(8,128)(2,1)} %get-tuple-element.89) | data formatting | bytes 8388608 | tf_op jit(solution)/shard_map/reshape;reshape | solution.py:44
  238.6 123.8 %all-gather.13.cloned.1.call-done = bf16[8192,2048]{1,0:T(8,128)(2,1)} async-done(((bf16[1024,2048]{1,0:T(8,128)(2,1)}), bf16[8192,2048]{1,0:T(8,128)(2,1)}) %all-gather.13.cloned.1.call-update) | async-done | bytes 33554448 | tf_op jit(solution)/shard_map/all_gather | solution.py:112
  362.4 14.2 %reduce_sum.53 = bf16[1024,2048]{1,0:T(8,128)(2,1)} reduce(bf16[8,1024,2048]{2,1,0:T(8,128)(2,1)} %bitcast.79, bf16[]{:T(256)} %constant.68.clone.1), dimensions={0}, to_apply=%region_7.8 | reduce | flops 14680064 | bytes 37748736 | tf_op jit(solution)/shard_map/reduce_sum | solution.py:112
  376.7 5.6 %fusion.23 = (f32[1024]{0:T(1024)S(1)}, bf16[1024,2048]{1,0:T(8,128)(2,1)S(1)}) fusion(bf16[1024,2048]{1,0:T(8,128)(2,1)} %reduce_sum.53, bf16[1024,2048]{1,0:T(8,128)(2,1)} %all-gather.7.cloned.1.call-done), kind=kLoop, calls=%fused_computation.34 | loop fusion | flops 14679040 | bytes 12587008 | tf_op jit(solution)/shard_map/reduce_sum | solution.py:14
  382.3 6.3 %fusion.45 = f32[1024,1024]{1,0:T(8,128)} fusion(bf16[2048,1024]{1,0:T(8,128)(2,1)S(1)} %copy-done.2, bf16[1024,2048]{1,0:T(8,128)(2,1)S(1)} %get-tuple-element.84, f32[2048]{0:T(1024)S(1)} %convert_element_type.101, f32[1024]{0:T(1024)S(1)} %add_rsqrt_fusion), kind=kOutput, calls=%fused_computation.54 | convolution fusion | flops 4303355904 | bytes 12595200 | tf_op jit(solution)/shard_map/dot_general | solution.py:120
  388.6 15.4 %convolution_convert_fusion.1 = bf16[1024,2048]{1,0:T(8,128)(2,1)} fusion(bf16[1024,2048]{0,1:T(8,128)(2,1)} %bitcast.86, f32[1024,1024]{1,0:T(8,128)} %fusion.45, bf16[2048,1024]{1,0:T(8,128)(2,1)} %reshape_reshape.7, bf16[1024,2048]{1,0:T(8,128)(2,1)} %copy-done, f32[2048]{0:T(1024)S(1)} %convert_element_type.101, f32[1024]{0:T(1024)S(1)} %add_rsqrt_fusion), kind=kOutput, calls=%fused_computation.51 | convolution fusion | flops 8606711808 | bytes 20983808 | tf_op jit(solution)/shard_map/dot_general | solution.py:123
  404.0 1.3 slice_bitcast_fusion.2
  407.4 35.6 %reduce-scatter.2.cloned.1.call-done = bf16[1024,256]{1,0:T(8,128)(2,1)} async-done(((bf16[1024,2048]{1,0:T(8,128)(2,1)}), bf16[1024,256]{1,0:T(8,128)(2,1)}) %reduce-scatter.2.cloned.1.call-update) | async-done | bytes 524304 | tf_op jit(solution)/shard_map/reduce_scatter | solution.py:124
  442.9 2.1 add_convert_fusion
  (52 shorter events, 11.0 us)
Async XLA Ops:
  7.2 7.4 %copy-start.7 = (bf16[2048]{0:T(1024)(128)(2,1)S(1)}, bf16[2048]{0:T(1024)(128)(2,1)}, u32[]{:S(2)}) copy-start(bf16[2048]{0:T(1024)(128)(2,1)} %param.16) | copy-start | bytes 12292
  7.2 41.0 %all-gather.7.cloned.1.call-start = ((), (), s32[]{:S(2)}) async-start(), calls=%async_computation.1 | async-start | bytes 4718592 | tf_op jit(solution)/shard_map/all_gather | solution.py:76
  7.9 96.8 %all-gather.9.cloned.1.call-start = ((), (), s32[]{:S(2)}) async-start(), calls=%async_computation.2 | async-start | bytes 3342336 | tf_op jit(solution)/shard_map/all_gather | solution.py:69
  9.7 191.8 %all-gather.11.cloned.1.call-start = ((), (), s32[]{:S(2)}) async-start(), calls=%async_computation.4 | async-start | bytes 14483456 | tf_op jit(solution)/shard_map/all_gather | solution.py:35
  13.9 348.5 %all-gather.13.cloned.1.call-start = ((), (), s32[]{:S(2)}) async-start(), calls=%async_computation.5 | async-start | bytes 37748736 | tf_op jit(solution)/shard_map/all_gather | solution.py:112
  111.3 1.8 copy-start.3
  112.3 1.4 copy-start.1
  116.8 4.2 copy-start.6
  129.4 2.6 copy-start.4
  135.0 1.0 copy-start.5
  206.7 0.7 copy-start.8
  206.8 236.2 %reduce-scatter.2.cloned.1.call-start = ((), (), s32[]{:S(2)}) async-start(), calls=%async_computation.3 | async-start | bytes 4718592 | tf_op jit(solution)/shard_map/reduce_scatter | solution.py:124
  376.7 5.6 %copy-start.2 = (bf16[2048,1024]{1,0:T(8,128)(2,1)S(1)}, bf16[2048,1024]{1,0:T(8,128)(2,1)}, u32[]{:S(2)}) copy-start(bf16[2048,1024]{1,0:T(8,128)(2,1)} %reshape_reshape.6) | copy-start | bytes 12582916
  382.3 6.4 %copy-start = (bf16[1024,2048]{1,0:T(8,128)(2,1)}, bf16[1024,2048]{1,0:T(8,128)(2,1)S(1)}, u32[]{:S(2)}) copy-start(bf16[1024,2048]{1,0:T(8,128)(2,1)S(1)} %get-tuple-element.84) | copy-start | bytes 12582916
Sparse Core Ops, SparseCore 0:
  9.7 38.4 all-gather.6
  50.9 53.7 all-gather.8
  106.9 94.6 all-gather.10
  206.9 155.4 all-gather.12
  404.1 38.7 reduce-scatter.1
